TPU v7x, 256 devices: a whole 4x4x8 slice. The times are simulated.
256 devices in a mesh: space: 16 (over x, z_hi), snap: 16 (over y, z_lo, core).
Axes of the slice: x: 4, y: 4, z: 8 (z_hi: 4, z_lo: 2; z = z_hi * 2 + z_lo), core: 2. Of those that a mesh axis runs over, the one named last changes fastest.
Arguments:
- velocity: bfloat16 [256, 3, 128, 32, 128], P('snap', None, 'space'), may hold values from -40 to 40
- phase_bins: int32 [256], replicated, may hold values from 0 to 23, as said below
- tile_owner: int32 [16], replicated, may hold values from 0 to 15, each once
Outputs:
- gram_tiles: float32 [16, 16, 256], P('space', None, 'snap')
Inputs may be any that keep to these rules, and one draw needn't show every extreme that they name: `phase_bins`: every bin holds at least one snapshot. `tile_owner`: each tile has exactly one owner.
All inputs are finite; a program needn't handle non-finite values.
Results may differ from a plain program's by a relative error of at most 0.0003.
Values may be sent and summed in bfloat16 or wider, within the bound.
No kernel may reach another device: no remote copies, remote signals or barrier semaphores. Data moves between devices by JAX's collectives and lax.ppermute only.
A program may use at most 128 MiB of HBM per device.

v0:
```python
import jax
import jax.numpy as jnp
from jax import lax
from jax.sharding import PartitionSpec as P

NB = 24


def with_halo(block, sides, width):
    for axis, dim in sides:
        count = lax.axis_size(axis)
        forward = [(i, i + 1) for i in range(count - 1)]
        backward = [(target, source) for source, target in forward]
        low = lax.ppermute(
            lax.slice_in_dim(block, block.shape[dim] - width, None, axis=dim), axis, forward
        )
        high = lax.ppermute(lax.slice_in_dim(block, 0, width, axis=dim), axis, backward)
        block = jnp.concatenate([low, block, high], axis=dim)
    return block


def widen(field_in, direction):
    widths = [(0, 0)] * field_in.ndim
    widths[direction] = (2, 2)
    return jnp.pad(field_in, widths)


def derivative(padded_field, direction):
    length = padded_field.shape[direction] - 4

    def window_at(offset):
        return lax.slice_in_dim(padded_field, offset, offset + length, axis=direction)

    return (8.0 * (window_at(3) - window_at(1)) - (window_at(4) - window_at(0))) / 12.0


def curl_field(u_field, v_field, w_field, v_wide, w_wide, first):
    second = first + 1
    third = first + 2
    omega_x = derivative(widen(w_field, second), second) - derivative(widen(v_field, third), third)
    omega_y = derivative(widen(u_field, third), third) - derivative(w_wide, first)
    omega_z = derivative(v_wide, first) - derivative(widen(u_field, second), second)
    return jnp.stack([omega_x, omega_y, omega_z], axis=first)


def per_device(velocity, phase_bins, tile_owner):
    widened = with_halo(velocity, (("space", 2),), 2).astype(jnp.float32)
    v_wide = widened[:, 1]
    w_wide = widened[:, 2]
    frame_float = velocity.astype(jnp.float32)
    vortex = curl_field(
        frame_float[:, 0], frame_float[:, 1], frame_float[:, 2], v_wide, w_wide, 1
    ).astype(jnp.bfloat16)
    snaps_dev, _, cells_x, cells_y, cells_z = vortex.shape
    flattened = vortex.reshape(snaps_dev, 3, cells_x * cells_y * cells_z)
    arranged = lax.all_to_all(flattened, "snap", split_axis=2, concat_axis=0, tiled=True)
    total_snaps = arranged.shape[0]
    columns = arranged.reshape(total_snaps, -1)
    onehot = (phase_bins[None, :] == jnp.arange(NB, dtype=jnp.int32)[:, None]).astype(jnp.bfloat16)
    bin_counts = jnp.sum(onehot.astype(jnp.float32), axis=1)
    bin_sums = jnp.dot(onehot, columns, preferred_element_type=jnp.float32)
    bin_means = bin_sums / bin_counts[:, None]
    fluctuation = (columns.astype(jnp.float32) - jnp.take(bin_means, phase_bins, axis=0)).astype(
        jnp.bfloat16
    )
    voxel_total = lax.axis_size("space") * cells_x * cells_y * cells_z
    partial_gram = (
        lax.dot_general(
            fluctuation, fluctuation, (((1,), (1,)), ((), ())), preferred_element_type=jnp.float32
        )
        / voxel_total
    )
    tile_count = lax.axis_size("space")
    tile_ids = jnp.arange(tile_count, dtype=jnp.int32)
    inverse = jnp.sum(
        tile_ids[None, :] * (tile_owner[None, :] == tile_ids[:, None]).astype(jnp.int32), axis=1
    )
    blocks = jnp.take(
        partial_gram.reshape(tile_count, total_snaps // tile_count, total_snaps), inverse, axis=0
    )
    rows_done = lax.psum_scatter(blocks, "space", scatter_dimension=0, tiled=True)
    return lax.psum_scatter(rows_done, "snap", scatter_dimension=2, tiled=True)


def solution(mesh):
    return jax.shard_map(
        per_device,
        mesh=mesh,
        in_specs=(P("snap", None, "space", None, None), P(), P()),
        out_specs=P("space", None, "snap"),
        check_vma=False,
    )
```

profile of v0, /device:TPU:2, one launch (start us, length us, event | category | flops | bytes accessed | tf_op | source)
XLA Modules:
  0.0 431.2 jit_solution(14037773328832607324)
XLA Ops:
  8.6 8.2 %collective-permute-start.1 = (bf16[16,3,2,32,128]{4,3,2,0,1:T(8,128)(2,1)}, bf16[16,3,2,32,128]{4,3,2,0,1:T(8,128)(2,1)}, u32[]{:S(2)}, u32[]{:S(2)}) collective-permute-start(bf16[16,3,2,32,128]{4,3,2,0,1:T(8,128)(2,1)} %copy.77), channel_id=1, source_target_pairs={{16,0},{32,16},{48,32},{64,48},{80,64},{96,80},{112,96},{128,112},... | collective-permute-start | bytes 2359304 | tf_op jit(solution)/shard_map/ppermute | solution.py:17
  16.8 2.1 slice.108
  21.7 2.4 slice_bitcast_fusion.1
  24.1 3.1 fusion.7
  27.2 2.3 stack.12
  29.5 21.3 %collective-permute-done.1 = bf16[16,3,2,32,128]{4,3,2,0,1:T(8,128)(2,1)} collective-permute-done((bf16[16,3,2,32,128]{4,3,2,0,1:T(8,128)(2,1)}, bf16[16,3,2,32,128]{4,3,2,0,1:T(8,128)(2,1)}, u32[]{:S(2)}, u32[]{:S(2)}) %collective-permute-start.1) | collective-permute-done | bytes 786464 | tf_op jit(solution)/shard_map/ppermute | solution.py:17
  50.8 8.6 %collective-permute-done = bf16[16,3,2,32,128]{4,3,2,1,0:T(8,128)(2,1)} collective-permute-done((bf16[16,3,2,32,128]{4,3,2,1,0:T(8,128)(2,1)}, bf16[16,3,2,32,128]{4,3,2,1,0:T(8,128)(2,1)}, u32[]{:S(2)}, u32[]{:S(2)}) %collective-permute-start) | collective-permute-done | bytes 786464 | tf_op jit(solution)/shard_map/ppermute | solution.py:14
  61.4 4.2 fusion.26
  68.2 2.2 pad_maximum_fusion
  70.3 31.0 %copy.55 = bf16[16,3,32768]{0,1,2:T(4,128)(2,1)} copy(bf16[16,3,32768]{2,0,1:T(8,128)(2,1)S(1)} %pad_maximum_fusion) | data formatting | bytes 6291456 | tf_op jit(solution)/shard_map/stack | solution.py:43
  101.3 29.5 %reshape.77 = bf16[16,2,49152]{2,1,0:T(2,128)(2,1)} reshape(bf16[32768,3,16]{2,1,0:T(4,128)(2,1)} %bitcast.45) | data formatting | bytes 6291456
  130.8 5.7 %all-to-all-start = ((bf16[16,2,49152]{2,1,0:T(2,128)(2,1)}), bf16[16,2,49152]{2,1,0:T(2,128)(2,1)S(1)}, u32[]{:S(2)}, u32[]{:S(2)}) async-start(bf16[16,2,49152]{2,1,0:T(2,128)(2,1)} %reshape.77), calls=%async_computation | async-start | bytes 6291456 | tf_op jit(solution)/shard_map/all_to_all | solution.py:56
  137.1 38.5 %all-to-all-done = bf16[16,2,49152]{2,1,0:T(2,128)(2,1)S(1)} async-done(((bf16[16,2,49152]{2,1,0:T(2,128)(2,1)}), bf16[16,2,49152]{2,1,0:T(2,128)(2,1)S(1)}, u32[]{:S(2)}, u32[]{:S(2)}) %all-to-all-start) | async-done | bytes 3145760 | tf_op jit(solution)/shard_map/all_to_all | solution.py:56
  175.6 32.7 %reshape.78 = bf16[32768,3,16]{2,1,0:T(4,128)(2,1)} reshape(bf16[16,2,49152]{2,1,0:T(2,128)(2,1)S(1)} %all-to-all-done) | data formatting | bytes 6291456
  208.3 30.1 %copy.61 = bf16[16,3,16,2048]{3,2,0,1:T(8,128)(2,1)S(1)} copy(bf16[16,3,16,2048]{0,1,3,2:T(4,128)(2,1)} %bitcast.46) | data formatting | bytes 6291456 | tf_op jit(solution)/shard_map/all_to_all | solution.py:56
  238.4 2.7 copy.58
  241.1 3.3 copy.66
  245.0 5.2 %gather_fusion = f32[256,6144]{1,0:T(8,128)} fusion(f32[24,6144]{1,0:T(8,128)S(1)} %convolution_divide_fusion, s32[1024]{0:T(1024)S(1)} %pad_clamp_fusion.1), kind=kCustom, calls=%fused_computation | custom fusion | bytes 12583936 | tf_op jit(solution)/shard_map/jit(_take)/gather | solution.py:63
  250.2 11.5 %gather.11 = f32[16,16,3,2048]{3,2,1,0:T(4,128)} reshape(f32[256,6144]{1,0:T(8,128)} %gather_fusion) | data formatting | bytes 12582912 | tf_op jit(solution)/shard_map/jit(_take)/gather | solution.py:63
  261.7 7.4 %fusion.1 = bf16[16,16,3,2048]{3,0,1,2:T(8,128)(2,1)S(1)} fusion(f32[16,16,3,2048]{3,2,1,0:T(4,128)} %gather.11, pred[16,16]{0,1:T(8,128)(4,1)S(1)} %copy.57, bf16[16,3,16,2048]{3,2,0,1:T(8,128)(2,1)S(1)} %copy-done.1), kind=kLoop, calls=%fused_computation.13 | loop fusion | flops 6291456 | bytes 12583168 | tf_op jit(solution)/shard_map/convert_element_type | solution.py:63
  269.1 2.7 copy.60
  271.8 3.3 copy.67
  277.6 80.9 %reduce-scatter.5.cloned.1.call-done = f32[1,16,256]{2,1,0:T(8,128)} async-done(((f32[16,16,256]{2,1,0:T(8,128)}), f32[1,16,256]{2,1,0:T(8,128)}) %reduce-scatter.5.cloned.1.call-update) | async-done | bytes 16400 | tf_op jit(solution)/shard_map/reduce_scatter | solution.py:81
  360.0 63.0 %reduce-scatter.7.cloned.1.call-done = f32[16,16]{1,0:T(8,128)} async-done(((f32[256,16]{1,0:T(8,128)}), f32[16,16]{1,0:T(8,128)}) %reduce-scatter.7.cloned.1.call-update) | async-done | bytes 1040
  (42 shorter events, 15.7 us)
Async XLA Ops:
  6.5 1.1 slice-start
  6.5 14.3 %copy-start.2 = (bf16[16,3,8,32,128]{4,3,2,1,0:T(8,128)(2,1)S(1)}, bf16[16,3,8,32,128]{4,3,2,1,0:T(8,128)(2,1)}, u32[]{:S(2)}) copy-start(bf16[16,3,8,32,128]{4,3,2,1,0:T(8,128)(2,1)} %param.3) | copy-start | bytes 9437188
  8.6 42.2 %collective-permute-start.1 = (bf16[16,3,2,32,128]{4,3,2,0,1:T(8,128)(2,1)}, bf16[16,3,2,32,128]{4,3,2,0,1:T(8,128)(2,1)}, u32[]{:S(2)}, u32[]{:S(2)}) collective-permute-start(bf16[16,3,2,32,128]{4,3,2,0,1:T(8,128)(2,1)} %copy.77), channel_id=1, source_target_pairs={{16,0},{32,16},{48,32},{64,48},{80,64},{96,80},{112,96},{128,112},... | collective-permute-start | bytes 2359304 | tf_op jit(solution)/shard_map/ppermute | solution.py:17
  18.9 40.5 %collective-permute-start = (bf16[16,3,2,32,128]{4,3,2,1,0:T(8,128)(2,1)}, bf16[16,3,2,32,128]{4,3,2,1,0:T(8,128)(2,1)}, u32[]{:S(2)}, u32[]{:S(2)}) collective-permute-start(bf16[16,3,2,32,128]{4,3,2,1,0:T(8,128)(2,1)} %slice.108), channel_id=1, source_target_pairs={{0,16},{16,32},{32,48},{48,64},{64,80},{80,96},{96,112},{112,128},... | collective-permute-start | bytes 2359304 | tf_op jit(solution)/shard_map/ppermute | solution.py:14
  24.1 35.3 %copy-start.3 = (bf16[16,3,8,32,128]{4,3,2,1,0:T(8,128)(2,1)S(1)}, bf16[16,3,8,32,128]{4,3,2,1,0:T(8,128)(2,1)}, u32[]{:S(2)}) copy-start(bf16[16,3,8,32,128]{4,3,2,1,0:T(8,128)(2,1)} %param.3) | copy-start | bytes 9437188
  29.5 31.9 %copy-start.4 = (f32[16,8,32,128]{3,2,1,0:T(8,128)S(1)}, f32[16,8,32,128]{3,2,1,0:T(8,128)}, u32[]{:S(2)}) copy-start(f32[16,8,32,128]{3,2,1,0:T(8,128)} %get-tuple-element.7) | copy-start | bytes 6291460
  130.8 5.8 %copy-start.5 = (s32[256]{0:T(256)S(1)}, s32[256]{0:T(256)}, u32[]{:S(2)}) copy-start(s32[256]{0:T(256)} %param.4) | copy-start | bytes 3076
  130.8 6.0 %copy-start.6 = (s32[16]{0:T(128)S(1)}, s32[16]{0:T(128)}, u32[]{:S(2)}) copy-start(s32[16]{0:T(128)} %param.5) | copy-start | bytes 196
  130.8 44.8 %all-to-all-start = ((bf16[16,2,49152]{2,1,0:T(2,128)(2,1)}), bf16[16,2,49152]{2,1,0:T(2,128)(2,1)S(1)}, u32[]{:S(2)}, u32[]{:S(2)}) async-start(bf16[16,2,49152]{2,1,0:T(2,128)(2,1)} %reshape.77), calls=%async_computation | async-start | bytes 6291456 | tf_op jit(solution)/shard_map/all_to_all | solution.py:56
  136.5 221.9 %reduce-scatter.5.cloned.1.call-start = ((), (), s32[]{:S(2)}) async-start(), calls=%async_computation.3 | async-start | bytes 278528 | tf_op jit(solution)/shard_map/reduce_scatter | solution.py:81
  238.4 2.7 copy-start
  250.2 11.5 %copy-start.1 = (bf16[16,3,16,2048]{3,2,0,1:T(8,128)(2,1)S(1)}, bf16[16,3,16,2048]{3,2,0,1:T(8,128)(2,1)}, u32[]{:S(2)}) copy-start(bf16[16,3,16,2048]{3,2,0,1:T(8,128)(2,1)} %copy-done) | copy-start | bytes 9437188
  277.5 145.5 %reduce-scatter.7.cloned.1.call-start = ((), (), s32[]{:S(2)}) async-start(), calls=%async_computation.4 | async-start | bytes 139264
Sparse Core Ops, SparseCore 0:
  277.6 80.8 reduce-scatter.4
  361.0 61.9 reduce-scatter.6
where the time goes:
time: 433 us; the launch traced here: 431 us
  waiting for transfers between devices  212 us (49%)
  local copies, waits for them, and re-layouts  167 us (39%)
  other arithmetic  20.8 us (5%)
  starting transfers between devices  15.9 us (4%)
  between operations  13.6 us (3%)
    reduce_scatter x1, waiting for transfers between devices, per_device(): lax.psum_scatter(blocks, 'space', scatter_dimension=0, tiled=True)  80.9 us
    unnamed x21, local copies, waits for them, and re-layouts  72.7 us
    unnamed x3, waiting for transfers between devices  63 us
    all_to_all x1, waiting for transfers between devices, per_device(): lax.all_to_all(flattened, 'snap', split_axis=2, concat_axis=0, tiled=True)  38.5 us
    another operation x4, local copies, waits for them, and re-layouts, curl_field(): return jnp.stack([omega_x, omega_y, omega_z], axis=first)  35.8 us
    all_to_all x2, local copies, waits for them, and re-layouts, per_device(): lax.all_to_all(flattened, 'snap', split_axis=2, concat_axis=0, tiled=True)  32.8 us
    ppermute x1, waiting for transfers between devices, with_halo(): lax.ppermute(lax.slice_in_dim(block, 0, width, axis=dim), axis, backward)  21.3 us
    gather x2, local copies, waits for them, and re-layouts, per_device(): jnp.take(bin_means, phase_bins, axis=0)  16.7 us
  transfers between devices with their start and end apart: 5, of which 5 were waited for; matrix products, arithmetic and copies ran while one was open for 3% of the time, Pallas kernels for 0%

commit v1 on v0

--- a/solution.py
+++ b/solution.py
@@ -53,7 +53,15 @@
     ).astype(jnp.bfloat16)
     snaps_dev, _, cells_x, cells_y, cells_z = vortex.shape
     flattened = vortex.reshape(snaps_dev, 3, cells_x * cells_y * cells_z)
-    arranged = lax.all_to_all(flattened, "snap", split_axis=2, concat_axis=0, tiled=True)
+    arranged = jnp.concatenate(
+        jax.lax.all_to_all(
+            jnp.stack(jnp.split(flattened, jax.lax.axis_size("snap"), axis=2), axis=0),
+            axis_name="snap",
+            split_axis=0,
+            concat_axis=0,
+        ),
+        axis=0,
+    )
     total_snaps = arranged.shape[0]
     columns = arranged.reshape(total_snaps, -1)
     onehot = (phase_bins[None, :] == jnp.arange(NB, dtype=jnp.int32)[:, None]).astype(jnp.bfloat16)

time: 433 us -> 325 us (0.75)
  local copies, waits for them, and re-layouts: 167 us -> 62.1 us
    unnamed x21 -> x36, local copies, waits for them, and re-layouts: 72.7 us -> 24.3 us
    all_to_all x2 -> x1, local copies, waits for them, and re-layouts: 32.8 us -> 2.75 us  [per_device(): jax.lax.all_to_all(jnp.stack(jnp.split(flattened, jax.lax.axis_size('snap...]
    another operation x4, local copies, waits for them, and re-layouts: 35.8 us -> 8.29 us  [curl_field(): return jnp.stack([omega_x, omega_y, omega_z], axis=first)]
    another operation x3 -> x2, other arithmetic: 9.54 us -> 8.11 us
  transfers between devices with their start and end apart: 5 -> 5, of which waited for: 5 -> 5; matrix products, arithmetic and copies ran while one was open for 3% -> 4% of each run, Pallas kernels for 0% -> 0%
where the time goes in v1:
time: 325 us; the launch traced here: 324 us
  waiting for transfers between devices  210 us (65%)
  local copies, waits for them, and re-layouts  62.1 us (19%)
  other arithmetic  20.7 us (6%)
  starting transfers between devices  16.1 us (5%)
  between operations  13.6 us (4%)
    reduce_scatter x1, waiting for transfers between devices, per_device(): lax.psum_scatter(blocks, 'space', scatter_dimension=0, tiled=True)  80.9 us
    unnamed x3, waiting for transfers between devices  62.8 us
    all_to_all x1, waiting for transfers between devices, per_device(): jax.lax.all_to_all(jnp.stack(jnp.split(flattened, jax.lax.axis_size('snap...  38.4 us
    unnamed x36, local copies, waits for them, and re-layouts  24.3 us
    ppermute x1, waiting for transfers between devices, with_halo(): lax.ppermute(lax.slice_in_dim(block, 0, width, axis=dim), axis, backward)  19 us
    gather x2, local copies, waits for them, and re-layouts, per_device(): jnp.take(bin_means, phase_bins, axis=0)  16.7 us
    convert_element_type x1, other arithmetic, per_device(): (columns.astype(jnp.float32) - jnp.take(bin_means, phase_bins, axis=0)).a...  8.68 us
    ppermute x1, waiting for transfers between devices, with_halo(): lax.ppermute(lax.slice_in_dim(block, block.shape[dim] - width, None, axis...  8.66 us
  transfers between devices with their start and end apart: 5, of which 5 were waited for; matrix products, arithmetic and copies ran while one was open for 4% of the time, Pallas kernels for 0%

profile of v1, /device:TPU:2, one launch (start us, length us, event | category | flops | bytes accessed | tf_op | source)
XLA Modules:
  0.0 323.8 jit_solution(7885252272439903787)
XLA Ops:
  8.8 8.2 %collective-permute-start.1 = (bf16[16,3,2,32,128]{4,3,2,0,1:T(8,128)(2,1)}, bf16[16,3,2,32,128]{4,3,2,0,1:T(8,128)(2,1)}, u32[]{:S(2)}, u32[]{:S(2)}) collective-permute-start(bf16[16,3,2,32,128]{4,3,2,0,1:T(8,128)(2,1)} %copy.56), channel_id=1, source_target_pairs={{16,0},{32,16},{48,32},{64,48},{80,64},{96,80},{112,96},{128,112},... | collective-permute-start | bytes 2359304 | tf_op jit(solution)/shard_map/ppermute | solution.py:17
  17.0 2.2 slice.108
  19.2 1.9 collective-permute-start
  21.9 2.4 slice_bitcast_fusion
  24.3 3.1 fusion.7
  27.4 2.3 stack.63
  29.7 2.3 constant_dynamic-update-slice_fusion.2
  32.0 19.0 %collective-permute-done.1 = bf16[16,3,2,32,128]{4,3,2,0,1:T(8,128)(2,1)} collective-permute-done((bf16[16,3,2,32,128]{4,3,2,0,1:T(8,128)(2,1)}, bf16[16,3,2,32,128]{4,3,2,0,1:T(8,128)(2,1)}, u32[]{:S(2)}, u32[]{:S(2)}) %collective-permute-start.1) | collective-permute-done | bytes 786464 | tf_op jit(solution)/shard_map/ppermute | solution.py:17
  51.0 8.7 %collective-permute-done = bf16[16,3,2,32,128]{4,3,2,1,0:T(8,128)(2,1)} collective-permute-done((bf16[16,3,2,32,128]{4,3,2,1,0:T(8,128)(2,1)}, bf16[16,3,2,32,128]{4,3,2,1,0:T(8,128)(2,1)}, u32[]{:S(2)}, u32[]{:S(2)}) %collective-permute-start) | collective-permute-done | bytes 786464 | tf_op jit(solution)/shard_map/ppermute | solution.py:14
  59.6 2.0 convert_bitcast_fusion.1
  61.7 5.0 %fusion.14 = (bf16[16,8,32,128]{3,2,1,0:T(8,128)(2,1)}, bf16[16,8,32,128]{3,2,1,0:T(8,128)(2,1)}) fusion(f32[16,8,32,128]{3,2,1,0:T(8,128)S(1)} %copy-done.3, f32[16,12,32,128]{3,2,1,0:T(8,128)S(1)} %get-tuple-element.8, f32[16,12,32,128]{3,2,1,0:T(8,128)S(1)} %get-tuple-element.9), kind=kLoop, calls=%fused_computation.36 | loop fusion | flops 12582912 | bytes 20971520 | tf_op jit(solution)/shard_map/convert.3
  66.7 2.4 stack.64
  69.1 2.3 stack.65
  85.0 5.7 %all-to-all-start = ((bf16[16,16,3,2048]{3,1,2,0:T(8,128)(2,1)}), bf16[16,16,3,2048]{3,1,2,0:T(8,128)(2,1)S(1)}, u32[]{:S(2)}, u32[]{:S(2)}) async-start(bf16[16,16,3,2048]{3,1,2,0:T(8,128)(2,1)} %fusion.34), calls=%async_computation | async-start | bytes 6291456 | tf_op jit(solution)/shard_map/all_to_all | solution.py:57
  91.4 38.4 %all-to-all-done = bf16[16,16,3,2048]{3,1,2,0:T(8,128)(2,1)S(1)} async-done(((bf16[16,16,3,2048]{3,1,2,0:T(8,128)(2,1)}), bf16[16,16,3,2048]{3,1,2,0:T(8,128)(2,1)S(1)}, u32[]{:S(2)}, u32[]{:S(2)}) %all-to-all-start) | async-done | bytes 3145760 | tf_op jit(solution)/shard_map/all_to_all | solution.py:57
  129.9 2.8 copy.38
  132.6 3.3 %copy.45 = bf16[32,8,3,2048]{3,1,2,0:T(8,128)(2,1)S(1)} copy(bf16[32,8,3,2048]{3,2,1,0:T(4,128)(2,1)S(1)} %bitcast.105) | data formatting | bytes 6291456
  136.5 5.2 %gather_fusion = f32[256,6144]{1,0:T(8,128)} fusion(f32[24,6144]{1,0:T(8,128)S(1)} %convolution_divide_fusion, s32[1024]{0:T(1024)S(1)} %get-tuple-element.13), kind=kCustom, calls=%fused_computation | custom fusion | bytes 12583936 | tf_op jit(solution)/shard_map/jit(_take)/gather | solution.py:71
  141.7 11.5 %gather.11 = f32[16,16,3,2048]{3,2,1,0:T(4,128)} reshape(f32[256,6144]{1,0:T(8,128)} %gather_fusion) | data formatting | bytes 12582912 | tf_op jit(solution)/shard_map/jit(_take)/gather | solution.py:71
  153.2 8.7 %fusion.1 = bf16[16,16,3,2048]{3,1,2,0:T(8,128)(2,1)S(1)} fusion(f32[16,16,3,2048]{3,2,1,0:T(4,128)} %gather.11, bf16[16,16,3,2048]{3,1,2,0:T(8,128)(2,1)S(1)} %copy-done.1, pred[16,16]{1,0:T(8,128)(4,1)S(1)} %broadcast_in_dim.31), kind=kLoop, calls=%fused_computation.13 | loop fusion | flops 6291456 | bytes 12583168 | tf_op jit(solution)/shard_map/convert_element_type | solution.py:71
  161.8 2.8 copy.40
  164.6 3.3 %copy.46 = bf16[32,8,3,2048]{3,1,2,0:T(8,128)(2,1)S(1)} copy(bf16[32,8,3,2048]{3,2,1,0:T(4,128)(2,1)S(1)} %bitcast.104) | data formatting | bytes 6291456
  170.4 80.9 %reduce-scatter.5.cloned.1.call-done = f32[1,16,256]{2,1,0:T(8,128)} async-done(((f32[16,16,256]{2,1,0:T(8,128)}), f32[1,16,256]{2,1,0:T(8,128)}) %reduce-scatter.5.cloned.1.call-update) | async-done | bytes 16400 | tf_op jit(solution)/shard_map/reduce_scatter | solution.py:89
  252.7 62.8 %reduce-scatter.7.cloned.1.call-done = f32[16,16]{1,0:T(8,128)} async-done(((f32[256,16]{1,0:T(8,128)}), f32[16,16]{1,0:T(8,128)}) %reduce-scatter.7.cloned.1.call-update) | async-done | bytes 1040
  (53 shorter events, 23.2 us)
Async XLA Ops:
  6.5 14.6 %copy-start.2 = (bf16[16,3,8,32,128]{4,3,2,1,0:T(8,128)(2,1)S(1)}, bf16[16,3,8,32,128]{4,3,2,1,0:T(8,128)(2,1)}, u32[]{:S(2)}) copy-start(bf16[16,3,8,32,128]{4,3,2,1,0:T(8,128)(2,1)} %param.3) | copy-start | bytes 9437188
  8.8 42.2 %collective-permute-start.1 = (bf16[16,3,2,32,128]{4,3,2,0,1:T(8,128)(2,1)}, bf16[16,3,2,32,128]{4,3,2,0,1:T(8,128)(2,1)}, u32[]{:S(2)}, u32[]{:S(2)}) collective-permute-start(bf16[16,3,2,32,128]{4,3,2,0,1:T(8,128)(2,1)} %copy.56), channel_id=1, source_target_pairs={{16,0},{32,16},{48,32},{64,48},{80,64},{96,80},{112,96},{128,112},... | collective-permute-start | bytes 2359304 | tf_op jit(solution)/shard_map/ppermute | solution.py:17
  19.2 40.5 %collective-permute-start = (bf16[16,3,2,32,128]{4,3,2,1,0:T(8,128)(2,1)}, bf16[16,3,2,32,128]{4,3,2,1,0:T(8,128)(2,1)}, u32[]{:S(2)}, u32[]{:S(2)}) collective-permute-start(bf16[16,3,2,32,128]{4,3,2,1,0:T(8,128)(2,1)} %slice.108), channel_id=1, source_target_pairs={{0,16},{16,32},{32,48},{48,64},{64,80},{80,96},{96,112},{112,128},... | collective-permute-start | bytes 2359304 | tf_op jit(solution)/shard_map/ppermute | solution.py:14
  32.0 29.7 %copy-start.3 = (f32[16,8,32,128]{3,2,1,0:T(8,128)S(1)}, f32[16,8,32,128]{3,2,1,0:T(8,128)}, u32[]{:S(2)}) copy-start(f32[16,8,32,128]{3,2,1,0:T(8,128)} %get-tuple-element.5) | copy-start | bytes 6291460
  66.6 4.7 %copy-start.4 = (bf16[16,3,32768]{2,0,1:T(8,128)(2,1)S(1)}, bf16[16,3,32768]{2,0,1:T(8,128)(2,1)}, u32[]{:S(2)}) copy-start(bf16[16,3,32768]{2,0,1:T(8,128)(2,1)} %constant_dynamic-update-slice_fusion.2) | copy-start | bytes 9437188
  85.0 6.0 %copy-start.5 = (s32[256]{0:T(256)S(1)}, s32[256]{0:T(256)}, u32[]{:S(2)}) copy-start(s32[256]{0:T(256)} %param.4) | copy-start | bytes 3076
  85.0 6.1 %copy-start.6 = (s32[16]{0:T(128)S(1)}, s32[16]{0:T(128)}, u32[]{:S(2)}) copy-start(s32[16]{0:T(128)} %param.5) | copy-start | bytes 196
  85.0 44.8 %all-to-all-start = ((bf16[16,16,3,2048]{3,1,2,0:T(8,128)(2,1)}), bf16[16,16,3,2048]{3,1,2,0:T(8,128)(2,1)S(1)}, u32[]{:S(2)}, u32[]{:S(2)}) async-start(bf16[16,16,3,2048]{3,1,2,0:T(8,128)(2,1)} %fusion.34), calls=%async_computation | async-start | bytes 6291456 | tf_op jit(solution)/shard_map/all_to_all | solution.py:57
  90.8 160.5 %reduce-scatter.5.cloned.1.call-start = ((), (), s32[]{:S(2)}) async-start(), calls=%async_computation.3 | async-start | bytes 278528 | tf_op jit(solution)/shard_map/reduce_scatter | solution.py:89
  129.8 2.8 copy-start
  141.7 11.5 %copy-start.1 = (bf16[16,16,3,2048]{3,1,2,0:T(8,128)(2,1)S(1)}, bf16[16,16,3,2048]{3,1,2,0:T(8,128)(2,1)}, u32[]{:S(2)}) copy-start(bf16[16,16,3,2048]{3,1,2,0:T(8,128)(2,1)} %copy-done) | copy-start | bytes 9437188
  170.3 145.2 %reduce-scatter.7.cloned.1.call-start = ((), (), s32[]{:S(2)}) async-start(), calls=%async_computation.4 | async-start | bytes 139264
Sparse Core Ops, SparseCore 0:
  170.5 80.7 reduce-scatter.4
  253.7 61.7 reduce-scatter.6
